TPU v7x, 256 devices: a whole 4x4x8 slice. The times are simulated.
256 devices in a mesh: ctx: 32 (over z, x), head: 8 (over y, core).
Axes of the slice: x: 4, y: 4, z: 8, core: 2. Of those that a mesh axis runs over, the one named last changes fastest.
Arguments:
- query_matrix: bfloat16 [32768, 4096], P(('ctx', 'head')), may hold values from -5 to 5
- key_matrix: bfloat16 [32768, 1024], P(('ctx', 'head')), may hold values from -5 to 5
- value_matrix: bfloat16 [32768, 1024], P(('ctx', 'head')), may hold values from -12 to 12
- output_gradient: bfloat16 [32768, 4096], P('ctx', 'head'), may hold values from -12 to 12
- doc_start: int32 [128], replicated, may hold values from 0 to 1, as said below
Outputs:
- attended: bfloat16 [32768, 4096], P('ctx', 'head')
- grad_q: bfloat16 [32768, 4096], P('ctx', 'head')
- grad_k: bfloat16 [32768, 1024], P('ctx', 'head')
- grad_v: bfloat16 [32768, 1024], P('ctx', 'head')
Inputs may be any that keep to these rules, and one draw needn't show every extreme that they name: `doc_start`: entry 0 is 1; a document starts at each unit whose entry is 1 and lasts to the next start or the end; every document has 1 to 4 units, and some document has exactly 1024 tokens.
All inputs are finite; a program needn't handle non-finite values.
Results may differ from a plain program's by a relative error of at most 0.019.
Values may be sent and summed in bfloat16 or wider, within the bound.
No kernel may reach another device: no remote copies, remote signals or barrier semaphores. Data moves between devices by JAX's collectives and lax.ppermute only.
A program may use at most 64 MiB of HBM per device.

v0:
```python
import jax
import jax.numpy as jnp
from jax import lax
from jax.sharding import PartitionSpec as P

QUERY_HEADS = 32
KEY_VALUE_HEADS = 8
HEAD_SIZE = 128


def from_behind(block, axis, distance):
    devices = range(lax.axis_size(axis))
    route = [(i - distance, i) for i in devices if i - distance in devices]
    return lax.ppermute(block, axis, route)


def tile_grads(query_tile, grad_tile, key_rows, value_rows, query_doc, key_doc, query_pos, key_pos):
    score_scale = query_tile.shape[-1] ** (-0.5)
    scores = (
        jnp.einsum("tgrd,ngd->grtn", query_tile, key_rows, preferred_element_type=jnp.float32)
        * score_scale
    )
    visible = (key_doc[None, :] == query_doc[:, None]) & (key_pos[None, :] <= query_pos[:, None])
    scores = jnp.where(visible, scores, -jnp.inf)
    row_top = jnp.max(scores, axis=-1, keepdims=True)
    log_total = row_top + jnp.log(jnp.sum(jnp.exp(scores - row_top), axis=-1, keepdims=True))
    weights = jnp.exp(scores - log_total)
    weights_low = weights.astype(jnp.bfloat16)
    attended = jnp.einsum(
        "grtn,ngd->tgrd", weights_low, value_rows, preferred_element_type=jnp.float32
    ).astype(jnp.bfloat16)
    row_delta = jnp.sum(grad_tile.astype(jnp.float32) * attended.astype(jnp.float32), axis=-1)
    row_delta = jnp.transpose(row_delta, (1, 2, 0))[..., None]
    grad_weights = jnp.einsum(
        "tgrd,ngd->grtn", grad_tile, value_rows, preferred_element_type=jnp.float32
    )
    grad_scores = (weights * (grad_weights - row_delta)).astype(jnp.bfloat16)
    grad_query = (
        jnp.einsum("grtn,ngd->tgrd", grad_scores, key_rows, preferred_element_type=jnp.float32)
        * score_scale
    ).astype(jnp.bfloat16)
    grad_key = (
        jnp.einsum("grtn,tgrd->ngd", grad_scores, query_tile, preferred_element_type=jnp.float32)
        * score_scale
    )
    grad_value = jnp.einsum(
        "grtn,tgrd->ngd", weights_low, grad_tile, preferred_element_type=jnp.float32
    )
    return (attended, grad_query, grad_key, grad_value)


def local(query_matrix, key_matrix, value_matrix, output_gradient, doc_start):
    token_per_shard = query_matrix.shape[0]
    head_groups = lax.axis_size("head")
    q_cols = query_matrix.shape[1] // head_groups
    k_cols = key_matrix.shape[1] // head_groups
    packed = jnp.concatenate(
        [
            query_matrix.reshape(token_per_shard, head_groups, q_cols),
            key_matrix.reshape(token_per_shard, head_groups, k_cols),
            value_matrix.reshape(token_per_shard, head_groups, k_cols),
        ],
        axis=2,
    )
    packed = lax.all_to_all(packed, "head", split_axis=1, concat_axis=0, tiled=True)
    ctx_rows = packed.shape[0]
    packed = packed.reshape(ctx_rows, q_cols + 2 * k_cols)
    kv_local = k_cols // HEAD_SIZE
    heads_per_group = q_cols // k_cols
    query_array = packed[:, :q_cols].reshape(ctx_rows, kv_local, heads_per_group, HEAD_SIZE)
    own_kv = packed[:, q_cols:]
    own_keys = own_kv[:, :k_cols].reshape(ctx_rows, kv_local, HEAD_SIZE)
    own_values = own_kv[:, k_cols:].reshape(ctx_rows, kv_local, HEAD_SIZE)
    unit_rows = 2 * token_per_shard
    earlier_kv = from_behind(own_kv, "ctx", 1)
    earlier_keys = earlier_kv[:, :k_cols].reshape(ctx_rows, kv_local, HEAD_SIZE)
    earlier_values = earlier_kv[:, k_cols:].reshape(ctx_rows, kv_local, HEAD_SIZE)
    gradient_per_head = output_gradient.reshape(ctx_rows, kv_local, heads_per_group, HEAD_SIZE)
    per_shard = ctx_rows // unit_rows
    ctx_index = lax.axis_index("ctx")
    unit_doc = jnp.cumsum(doc_start)
    own_units = lax.dynamic_slice_in_dim(unit_doc, ctx_index * per_shard, per_shard)
    prior_units = lax.dynamic_slice_in_dim(
        unit_doc, jnp.maximum(ctx_index - 1, 0) * per_shard, per_shard
    )
    prior_units = jnp.where(ctx_index > 0, prior_units, -1)
    own_doc = jnp.repeat(own_units, unit_rows, total_repeat_length=ctx_rows)
    prior_doc = jnp.repeat(prior_units, unit_rows, total_repeat_length=ctx_rows)
    joined_keys = jnp.concatenate([earlier_keys, own_keys], axis=0)
    joined_values = jnp.concatenate([earlier_values, own_values], axis=0)
    joined_doc = jnp.concatenate([prior_doc, own_doc], axis=0)
    joined_pos = jnp.arange(ctx_rows + ctx_rows, dtype=jnp.int32) - ctx_rows
    before = ctx_rows - unit_rows
    key_grad = jnp.zeros((ctx_rows + ctx_rows, kv_local, HEAD_SIZE), jnp.float32)
    value_grad = jnp.zeros((ctx_rows + ctx_rows, kv_local, HEAD_SIZE), jnp.float32)
    pieces = []
    query_grads = []
    for unit_number in range(per_shard):
        first_row = unit_number * unit_rows
        end_row = first_row + unit_rows
        window_start = ctx_rows - before + first_row
        window_end = window_start + ctx_rows
        query_tile = query_array[first_row:end_row]
        grad_tile = gradient_per_head[first_row:end_row]
        query_doc = own_doc[first_row:end_row]
        query_pos = jnp.arange(first_row, end_row, dtype=jnp.int32)
        results = tile_grads(
            query_tile,
            grad_tile,
            joined_keys[window_start:window_end],
            joined_values[window_start:window_end],
            query_doc,
            joined_doc[window_start:window_end],
            query_pos,
            joined_pos[window_start:window_end],
        )
        attended, grad_query, grad_key, grad_value = results
        pieces.append(attended)
        query_grads.append(grad_query)
        key_grad = key_grad.at[window_start:window_end].add(grad_key)
        value_grad = value_grad.at[window_start:window_end].add(grad_value)
    prior_grads = jnp.concatenate(
        [
            key_grad[:ctx_rows].astype(jnp.bfloat16).reshape(ctx_rows, k_cols),
            value_grad[:ctx_rows].astype(jnp.bfloat16).reshape(ctx_rows, k_cols),
        ],
        axis=1,
    )
    later = from_behind(prior_grads, "ctx", -1).astype(jnp.float32)
    key_own = key_grad[ctx_rows:].reshape(ctx_rows, k_cols) + later[:, :k_cols]
    value_own = value_grad[ctx_rows:].reshape(ctx_rows, k_cols) + later[:, k_cols:]
    summed_keys = key_own.astype(jnp.bfloat16)
    summed_values = value_own.astype(jnp.bfloat16)
    attended_all = jnp.concatenate(pieces, axis=0).reshape(
        ctx_rows, kv_local * heads_per_group * HEAD_SIZE
    )
    query_total = jnp.concatenate(query_grads, axis=0).reshape(
        ctx_rows, kv_local * heads_per_group * HEAD_SIZE
    )
    return (attended_all, query_total, summed_keys, summed_values)


def solution(mesh):
    placed = (
        P(("ctx", "head"), None),
        P(("ctx", "head"), None),
        P(("ctx", "head"), None),
        P("ctx", "head"),
        P(),
    )
    return jax.shard_map(
        local,
        mesh=mesh,
        in_specs=placed,
        out_specs=(P("ctx", "head"), P("ctx", "head"), P("ctx", "head"), P("ctx", "head")),
        check_vma=False,
    )
```

profile of v0, /device:TPU:102, one launch (start us, length us, event | category | flops | bytes accessed | tf_op | source)
XLA Modules:
  0.0 101.2 jit_solution(3459865520196995552)
XLA Ops:
  0.6 1.4 %copy.156 = bf16[16,8,8,512]{3,2,0,1:T(8,128)(2,1)S(1)} copy(bf16[16,8,8,512]{3,2,1,0:T(8,128)(2,1)} %bitcast.542) | data formatting | bytes 2097152 | tf_op jit(solution)/shard_map/reshape | solution.py:59
  2.0 1.2 %copy_bitcast_fusion.1 = (bf16[128,8,128]{2,0,1:T(8,128)(2,1)S(1)}, bf16[128,8,128]{2,0,1:T(8,128)(2,1)S(1)}) fusion(bf16[128,1024]{1,0:T(8,128)(2,1)S(1)} %copy-done, bf16[128,1024]{1,0:T(8,128)(2,1)} %param.29), kind=kLoop, calls=%fused_computation.142 | loop fusion | bytes 1048576 | tf_op jit(solution)/shard_map/reshape | solution.py:61
  3.3 1.3 %pad_maximum_fusion = bf16[128,8,768]{2,0,1:T(8,128)(2,1)} fusion(bf16[128,8,128]{2,0,1:T(8,128)(2,1)S(1)} %get-tuple-element.184, bf16[128,8,128]{2,0,1:T(8,128)(2,1)S(1)} %get-tuple-element.185, bf16[128,8,512]{2,0,1:T(8,128)(2,1)S(1)} %bitcast.535), kind=kLoop, calls=%fused_computation.52 | loop fusion | flops 4718592 | bytes 3145728 | tf_op jit(solution)/shard_map/concatenate | solution.py:57
  4.5 4.5 %all-to-all-start = ((bf16[128,8,768]{2,0,1:T(8,128)(2,1)}), bf16[128,8,768]{2,0,1:T(8,128)(2,1)S(1)}, u32[]{:S(2)}, u32[]{:S(2)}) async-start(bf16[128,8,768]{2,0,1:T(8,128)(2,1)} %pad_maximum_fusion), calls=%async_computation | async-start | bytes 3145728 | tf_op jit(solution)/shard_map/all_to_all | solution.py:65
  9.2 0.2 reduce-window.9
  9.3 0.9 fusion.196
  10.2 0.1 select_reduce_fusion
  10.4 0.7 fusion.199
  11.1 5.0 %select_select_fusion.1 = (s32[1024]{0:T(1024)S(1)}, s32[1024]{0:T(1024)S(1)}) fusion(pred[1024]{0:T(1024)(128)(4,1)S(1)} %copy-done.12, pred[1024]{0:T(1024)(128)(4,1)S(1)} %copy-done.13, pred[1024]{0:T(1024)(128)(4,1)S(1)} %copy-done.14, s32[]{:T(128)} %bitcast.13, s32[]{:T(128)} %bitcast.12, s32[]{:T(128)} %bitcast.11, s32[]{:T(128)} %bitcast.10, ...), kind=kLoop, calls=%fused_computation.171 | loop fusion | flops 6144 | bytes 11296 | tf_op jit(solution)/shard_map/jit(_take)/gather | solution.py:88
  16.1 1.8 %copy.143 = bf16[256,512]{0,1:T(8,128)(2,1)} copy(bf16[256,512]{1,0:T(8,128)(2,1)} %get-tuple-element.137) | data formatting | bytes 524288
  17.9 1.8 %copy.144 = bf16[256,512]{0,1:T(8,128)(2,1)} copy(bf16[256,512]{1,0:T(8,128)(2,1)} %get-tuple-element.139) | data formatting | bytes 524288
  19.7 0.9 copy.145
  20.6 0.8 copy.146
  21.5 0.3 fusion.136
  21.8 0.3 compare_and_fusion
  22.1 0.3 compare_and_fusion.2
  22.5 0.3 compare_and_fusion.1
  22.8 7.7 %all-to-all-done = bf16[128,8,768]{2,0,1:T(8,128)(2,1)S(1)} async-done(((bf16[128,8,768]{2,0,1:T(8,128)(2,1)}), bf16[128,8,768]{2,0,1:T(8,128)(2,1)S(1)}, u32[]{:S(2)}, u32[]{:S(2)}) %all-to-all-start) | async-done | bytes 1572896 | tf_op jit(solution)/shard_map/all_to_all | solution.py:65
  30.6 0.8 slice.388
  31.4 0.9 fusion.195
  32.3 5.1 %collective-permute-start = (bf16[1024,256]{1,0:T(8,128)(2,1)}, bf16[1024,256]{1,0:T(8,128)(2,1)}, u32[]{:S(2)}, u32[]{:S(2)}) collective-permute-start(bf16[1024,256]{1,0:T(8,128)(2,1)} %slice.388), channel_id=1, source_target_pairs={{0,8},{8,16},{16,24},{24,32},{32,40},{40,48},{48,56},{56,64},{64,7... | collective-permute-start | bytes 1572872 | tf_op jit(solution)/shard_map/ppermute | solution.py:14
  37.4 1.1 %copy.149 = bf16[256,512]{0,1:T(8,128)(2,1)S(1)} copy(bf16[256,512]{1,0:T(8,128)(2,1)} %get-tuple-element.132) | data formatting | bytes 524288 | tf_op jit(solution)/shard_map/reshape.306
  38.5 0.8 fusion.15
  39.3 0.9 exponential_reduce_fusion
  40.2 1.9 %fusion.141 = (f32[256,4]{0,1:T(4,128)S(1)}, bf16[256,1,4,128]{0,3,2,1:T(8,128)(2,1)}) fusion(bf16[256,1,4,128]{0,3,2,1:T(8,128)(2,1)S(1)} %bitcast.547, f32[1024,256,4]{1,0,2:T(8,128)S(1)} %get-tuple-element.165, f32[4,256]{1,0:T(4,128)S(1)} %log_add_fusion, pred[256,1024]{0,1:T(8,128)(4,1)S(1)} %compare_and_fusion, bf16[1024,768]{1,0:T(8,128)(2,1)S(1)} %bitcast.531), kind=kOutput, calls=%fused_computation.125 | convolution fusion | flops 273284096 | bytes 5251072 | tf_op jit(solution)/shard_map/grtn,ngd->tgrd/dot_general | solution.py:29
  42.2 2.7 %fusion.1 = bf16[1,4,256,1024]{2,3,1,0:T(8,128)(2,1)} fusion(f32[1024,256,4]{1,0,2:T(8,128)S(1)} %get-tuple-element.165, bf16[256,4,128]{0,2,1:T(8,128)(2,1)S(1)} %bitcast.548, f32[4,256]{1,0:T(4,128)S(1)} %bitcast.562, f32[4,256]{1,0:T(4,128)S(1)} %log_add_fusion, pred[256,1024]{0,1:T(8,128)(4,1)S(1)} %compare_and_fusion, bf16[1024,768]{1,0:T(8,128)(2,1)S(1)} %bitcast.532), kind=kOutput, calls=%fused_computation.2 | convolution fusion | flops 274726912 | bytes 7086080 | tf_op jit(solution)/shard_map/tgrd,ngd->grtn/dot_general | solution.py:34
  44.8 1.8 %copy.59 = bf16[256,512]{0,1:T(8,128)(2,1)} copy(bf16[256,512]{1,0:T(8,128)(2,1)} %get-tuple-element.131) | data formatting | bytes 524288 | tf_op jit(solution)/shard_map/slice | solution.py:103
  46.6 0.8 copy.147
  47.4 1.1 %copy.148 = bf16[256,512]{0,1:T(8,128)(2,1)S(1)} copy(bf16[256,512]{1,0:T(8,128)(2,1)} %get-tuple-element.133) | data formatting | bytes 524288 | tf_op jit(solution)/shard_map/reshape.297
  48.5 2.1 %fusion.129 = bf16[256,1,4,128]{0,3,2,1:T(8,128)(2,1)S(1)} fusion(bf16[1,4,256,1024]{2,3,1,0:T(8,128)(2,1)} %fusion.1, bf16[1024,768]{1,0:T(8,128)(2,1)S(1)} %bitcast.533), kind=kOutput, calls=%fused_computation.96 | convolution fusion | flops 268697600 | bytes 2621440 | tf_op jit(solution)/shard_map/grtn,ngd->tgrd/dot_general | solution.py:39
  50.7 1.1 %slice_bitcast_fusion = (bf16[1024,1,128]{2,0,1:T(8,128)(2,1)S(1)}, bf16[1024,1,128]{2,0,1:T(8,128)(2,1)S(1)}) fusion(bf16[1024,256]{1,0:T(8,128)(2,1)} %collective-permute-done), kind=kLoop, calls=%fused_computation.148 | loop fusion | bytes 1048576 | tf_op jit(solution)/shard_map/reshape | solution.py:76
  51.8 0.8 fusion.12
  52.6 0.9 exponential_reduce_fusion.3
  53.5 1.3 %convolution_bitcast_fusion.3 = f32[1024,1,128]{0,2,1:T(8,128)S(1)} fusion(bf16[256,4,128]{0,2,1:T(8,128)(2,1)S(1)} %bitcast.556, f32[1024,256,4]{1,0,2:T(8,128)S(1)} %get-tuple-element.171, f32[4,256]{1,0:T(4,128)S(1)} %log_add_fusion.3, pred[256,1024]{0,1:T(8,128)(4,1)S(1)} %fusion.136), kind=kOutput, calls=%fused_computation.60 | convolution fusion | flops 272629760 | bytes 5246976 | tf_op jit(solution)/shard_map/grtn,tgrd->ngd/dot_general | solution.py:46
  54.8 1.9 %fusion.144 = (f32[256,4]{0,1:T(4,128)S(1)}, bf16[256,1,4,128]{0,3,2,1:T(8,128)(2,1)}) fusion(bf16[256,1,4,128]{0,3,2,1:T(8,128)(2,1)S(1)} %bitcast.557, f32[1024,256,4]{1,0,2:T(8,128)S(1)} %get-tuple-element.171, f32[4,256]{1,0:T(4,128)S(1)} %log_add_fusion.3, pred[256,1024]{0,1:T(8,128)(4,1)S(1)} %fusion.136, ...), kind=kOutput, calls=%fused_computation.131 | convolution fusion | flops 273808384 | bytes 5513216 | tf_op jit(solution)/shard_map/grtn,ngd->tgrd/dot_general | solution.py:29
  56.7 1.3 %fusion.7 = bf16[1,4,256,1024]{2,3,1,0:T(8,128)(2,1)S(1)} fusion(f32[1024,256,4]{1,0,2:T(8,128)S(1)} %get-tuple-element.171, bf16[256,4,128]{0,2,1:T(8,128)(2,1)S(1)} %bitcast.558, f32[4,256]{1,0:T(4,128)S(1)} %bitcast.560, f32[4,256]{1,0:T(4,128)S(1)} %log_add_fusion.3, pred[256,1024]{0,1:T(8,128)(4,1)S(1)} %fusion.136, ...), kind=kOutput, calls=%fused_computation.11 | convolution fusion | flops 275251200 | bytes 7348224 | tf_op jit(solution)/shard_map/tgrd,ngd->grtn/dot_general | solution.py:34
  58.1 0.8 fusion.87
  58.9 0.5 fusion.120
  59.4 0.8 fusion.13
  60.2 1.1 %exponential_reduce_fusion.2 = f32[4,256]{1,0:T(4,128)S(1)} fusion(f32[1024,256,4]{1,0,2:T(8,128)S(1)} %get-tuple-element.169, f32[4,256]{1,0:T(4,128)S(1)} %get-tuple-element.168, pred[256,1024]{0,1:T(8,128)(4,1)S(1)} %compare_and_fusion.2), kind=kLoop, calls=%fused_computation.21 | loop fusion | flops 4193280 | bytes 4464640 | tf_op jit(solution)/shard_map/reduce_sum | solution.py:26
  61.3 0.8 fusion.14
  62.1 0.9 exponential_reduce_fusion.1
  63.2 1.9 %fusion.143 = (f32[256,4]{0,1:T(4,128)S(1)}, bf16[256,1,4,128]{0,3,2,1:T(8,128)(2,1)}) fusion(bf16[256,1,4,128]{0,3,2,1:T(8,128)(2,1)S(1)} %bitcast.553, f32[1024,256,4]{1,0,2:T(8,128)S(1)} %get-tuple-element.169, f32[4,256]{1,0:T(4,128)S(1)} %log_add_fusion.2, pred[256,1024]{0,1:T(8,128)(4,1)S(1)} %compare_and_fusion.2, ...), kind=kOutput, calls=%fused_computation.129 | convolution fusion | flops 273808384 | bytes 5513216 | tf_op jit(solution)/shard_map/grtn,ngd->tgrd/dot_general | solution.py:29
  65.1 1.3 %fusion.5 = bf16[1,4,256,1024]{2,3,1,0:T(8,128)(2,1)S(1)} fusion(f32[1024,256,4]{1,0,2:T(8,128)S(1)} %get-tuple-element.169, bf16[256,4,128]{0,2,1:T(8,128)(2,1)S(1)} %bitcast.554, f32[4,256]{1,0:T(4,128)S(1)} %bitcast.563, f32[4,256]{1,0:T(4,128)S(1)} %log_add_fusion.2, pred[256,1024]{0,1:T(8,128)(4,1)S(1)} %compare_and_fusion.2, ...), kind=kOutput, calls=%fused_computation.8 | convolution fusion | flops 275251200 | bytes 7348224 | tf_op jit(solution)/shard_map/tgrd,ngd->grtn/dot_general | solution.py:34
  66.4 0.9 fusion.93
  67.3 1.9 %fusion.142 = (f32[256,4]{0,1:T(4,128)S(1)}, bf16[256,1,4,128]{0,3,2,1:T(8,128)(2,1)}) fusion(bf16[256,1,4,128]{0,3,2,1:T(8,128)(2,1)S(1)} %bitcast.550, f32[1024,256,4]{1,0,2:T(8,128)S(1)} %get-tuple-element.167, f32[4,256]{1,0:T(4,128)S(1)} %log_add_fusion.1, pred[256,1024]{0,1:T(8,128)(4,1)S(1)} %compare_and_fusion.1, ...), kind=kOutput, calls=%fused_computation.127 | convolution fusion | flops 273808384 | bytes 5513216 | tf_op jit(solution)/shard_map/grtn,ngd->tgrd/dot_general | solution.py:29
  69.2 1.3 %fusion.3 = bf16[1,4,256,1024]{2,3,1,0:T(8,128)(2,1)S(1)} fusion(f32[1024,256,4]{1,0,2:T(8,128)S(1)} %get-tuple-element.167, bf16[256,4,128]{0,2,1:T(8,128)(2,1)S(1)} %bitcast.551, f32[4,256]{1,0:T(4,128)S(1)} %bitcast.561, f32[4,256]{1,0:T(4,128)S(1)} %log_add_fusion.1, pred[256,1024]{0,1:T(8,128)(4,1)S(1)} %compare_and_fusion.1, ...), kind=kOutput, calls=%fused_computation.5 | convolution fusion | flops 275251200 | bytes 7348224 | tf_op jit(solution)/shard_map/tgrd,ngd->grtn/dot_general | solution.py:34
  70.5 0.9 fusion.99
  71.5 1.4 %fusion.49 = f32[2048,1,128]{0,2,1:T(8,128)S(1)} fusion(f32[2048,1,128]{0,2,1:T(8,128)S(1)} %scatter-add.25, bf16[256,4,128]{0,2,1:T(8,128)(2,1)S(1)} %bitcast.555, f32[1024,256,4]{1,0,2:T(8,128)S(1)} %get-tuple-element.169, f32[4,256]{1,0:T(4,128)S(1)} %log_add_fusion.2, pred[256,1024]{0,1:T(8,128)(4,1)S(1)} %compare_and_fusion.2), kind=kOutput, calls=%fused_computation.62 | convolution fusion | flops 272760832 | bytes 5771264 | tf_op jit(solution)/shard_map/grtn,tgrd->ngd/dot_general | solution.py:46
  72.9 1.4 %fusion.51 = f32[2048,1,128]{0,2,1:T(8,128)S(1)} fusion(f32[2048,1,128]{0,2,1:T(8,128)S(1)} %fusion.49, bf16[256,4,128]{0,2,1:T(8,128)(2,1)S(1)} %bitcast.552, f32[1024,256,4]{1,0,2:T(8,128)S(1)} %get-tuple-element.167, f32[4,256]{1,0:T(4,128)S(1)} %log_add_fusion.1, pred[256,1024]{0,1:T(8,128)(4,1)S(1)} %compare_and_fusion.1), kind=kOutput, calls=%fused_computation.64 | convolution fusion | flops 272760832 | bytes 5771264 | tf_op jit(solution)/shard_map/grtn,tgrd->ngd/dot_general | solution.py:46
  74.3 0.9 pad_maximum_fusion.3
  75.3 2.2 %collective-permute-start.1 = (bf16[1024,256]{0,1:T(8,128)(2,1)}, bf16[1024,256]{0,1:T(8,128)(2,1)}, u32[]{:S(2)}, u32[]{:S(2)}) collective-permute-start(bf16[1024,256]{0,1:T(8,128)(2,1)} %pad_maximum_fusion.3), channel_id=1, source_target_pairs={{8,0},{16,8},{24,16},{32,24},{40,32},{48,40},{56,48},{64,56},{72,6... | collective-permute-start | bytes 1572872 | tf_op jit(solution)/shard_map/ppermute | solution.py:14
  77.5 0.5 fusion.126
  77.9 0.5 fusion.123
  78.4 0.1 pad_maximum_fusion.2
  78.6 1.3 %copy.101 = bf16[1024,512]{1,0:T(8,128)(2,1)} copy(bf16[1024,512]{0,1:T(8,128)(2,1)S(1)} %bitcast.536) | data formatting | bytes 2097152
  79.9 1.3 %pad_maximum_fusion.1 = bf16[1024,1,4,128]{0,3,2,1:T(8,128)(2,1)S(1)} fusion(bf16[256,1,4,128]{0,3,2,1:T(8,128)(2,1)} %get-tuple-element.173, bf16[256,1,4,128]{0,3,2,1:T(8,128)(2,1)} %get-tuple-element.175, bf16[256,1,4,128]{0,3,2,1:T(8,128)(2,1)} %get-tuple-element.177, bf16[256,1,4,128]{0,3,2,1:T(8,128)(2,1)} %get-tuple-element.179), kind=kLoop, calls=%fused_computation.102 | loop fusion | flops 4194304 | bytes 2097152 | tf_op jit(solution)/shard_map/concatenate | solution.py:134
  81.2 1.3 %copy.100 = bf16[1024,512]{1,0:T(8,128)(2,1)} copy(bf16[1024,512]{0,1:T(8,128)(2,1)S(1)} %bitcast.537) | data formatting | bytes 2097152
  82.6 11.4 %collective-permute-done.1 = bf16[1024,256]{0,1:T(8,128)(2,1)} collective-permute-done((bf16[1024,256]{0,1:T(8,128)(2,1)}, bf16[1024,256]{0,1:T(8,128)(2,1)}, u32[]{:S(2)}, u32[]{:S(2)}) %collective-permute-start.1) | collective-permute-done | bytes 524320 | tf_op jit(solution)/shard_map/ppermute | solution.py:14
  93.9 1.1 %convert_element_type.219 = f32[1024,256]{0,1:T(8,128)S(1)} convert(bf16[1024,256]{0,1:T(8,128)(2,1)} %collective-permute-done.1) | non-fusion elementwise | flops 262144 | bytes 1572864 | tf_op jit(solution)/shard_map/convert_element_type | solution.py:129
  95.1 3.6 %fusion.137 = bf16[1024,128]{0,1:T(8,128)(2,1)S(1)} fusion(f32[1024,256]{0,1:T(8,128)S(1)} %convert_element_type.219, bf16[256,4,128]{0,2,1:T(8,128)(2,1)S(1)} %bitcast.549, f32[2048,1,128]{0,2,1:T(8,128)} %copy-done.3, f32[1024,256,4]{1,0,2:T(8,128)} %copy-done.1, f32[4,256]{1,0:T(4,128)S(1)} %log_add_fusion, pred[256,1024]{0,1:T(8,128)(4,1)S(1)} %compare_and_fusion), kind=kOutput, calls=%fused_computation.118 | convolution fusion | flops 273022976 | bytes 6033408 | tf_op jit(solution)/shard_map/grtn,tgrd->ngd/dot_general | solution.py:46
  98.7 0.8 fusion.138
  99.5 0.8 copy.103
  100.4 0.8 copy.102
  (50 shorter events, 0.6 us)
Async XLA Ops:
  0.6 1.4 %copy-start = (bf16[128,1024]{1,0:T(8,128)(2,1)S(1)}, bf16[128,1024]{1,0:T(8,128)(2,1)}, u32[]{:S(2)}) copy-start(bf16[128,1024]{1,0:T(8,128)(2,1)} %param.28) | copy-start | bytes 786436
  2.0 7.0 %copy-start.15 = (s32[128]{0:T(128)S(1)}, s32[128]{0:T(128)}, u32[]{:S(2)}) copy-start(s32[128]{0:T(128)} %param.31) | copy-start | bytes 1540
  2.0 7.3 %copy-start.4 = (bf16[1024,512]{1,0:T(8,128)(2,1)S(1)}, bf16[1024,512]{1,0:T(8,128)(2,1)}, u32[]{:S(2)}) copy-start(bf16[1024,512]{1,0:T(8,128)(2,1)} %param.30) | copy-start | bytes 3145732
  3.2 7.9 %copy-start.12 = (pred[1024]{0:T(1024)(128)(4,1)S(1)}, pred[1024]{0:T(1024)(128)(4,1)}, u32[]{:S(2)}) copy-start(pred[1024]{0:T(1024)(128)(4,1)} %constant.343) | copy-start | bytes 3076
  3.2 7.8 %copy-start.13 = (pred[1024]{0:T(1024)(128)(4,1)S(1)}, pred[1024]{0:T(1024)(128)(4,1)}, u32[]{:S(2)}) copy-start(pred[1024]{0:T(1024)(128)(4,1)} %constant.344) | copy-start | bytes 3076
  3.2 7.8 %copy-start.14 = (pred[1024]{0:T(1024)(128)(4,1)S(1)}, pred[1024]{0:T(1024)(128)(4,1)}, u32[]{:S(2)}) copy-start(pred[1024]{0:T(1024)(128)(4,1)} %constant.345) | copy-start | bytes 3076
  4.5 26.0 %all-to-all-start = ((bf16[128,8,768]{2,0,1:T(8,128)(2,1)}), bf16[128,8,768]{2,0,1:T(8,128)(2,1)S(1)}, u32[]{:S(2)}, u32[]{:S(2)}) async-start(bf16[128,8,768]{2,0,1:T(8,128)(2,1)} %pad_maximum_fusion), calls=%async_computation | async-start | bytes 3145728 | tf_op jit(solution)/shard_map/all_to_all | solution.py:65
  32.3 18.4 %collective-permute-start = (bf16[1024,256]{1,0:T(8,128)(2,1)}, bf16[1024,256]{1,0:T(8,128)(2,1)}, u32[]{:S(2)}, u32[]{:S(2)}) collective-permute-start(bf16[1024,256]{1,0:T(8,128)(2,1)} %slice.388), channel_id=1, source_target_pairs={{0,8},{8,16},{16,24},{24,32},{32,40},{40,48},{48,56},{56,64},{64,7... | collective-permute-start | bytes 1572872 | tf_op jit(solution)/shard_map/ppermute | solution.py:14
  38.5 1.7 %copy-start.7 = (bf16[256,512]{0,1:T(8,128)(2,1)S(1)}, bf16[256,512]{0,1:T(8,128)(2,1)}, u32[]{:S(2)}) copy-start(bf16[256,512]{0,1:T(8,128)(2,1)} %copy.146) | copy-start | bytes 786436
  39.3 2.9 %copy-start.1 = (f32[1024,256,4]{1,0,2:T(8,128)}, f32[1024,256,4]{1,0,2:T(8,128)S(1)}, u32[]{:S(2)}) copy-start(f32[1024,256,4]{1,0,2:T(8,128)S(1)} %get-tuple-element.165) | copy-start | bytes 12582916
  48.5 3.2 %copy-start.6 = (bf16[256,512]{0,1:T(8,128)(2,1)S(1)}, bf16[256,512]{0,1:T(8,128)(2,1)}, u32[]{:S(2)}) copy-start(bf16[256,512]{0,1:T(8,128)(2,1)} %copy.59) | copy-start | bytes 786436
  51.8 1.7 %copy-start.11 = (bf16[256,512]{0,1:T(8,128)(2,1)S(1)}, bf16[256,512]{0,1:T(8,128)(2,1)}, u32[]{:S(2)}) copy-start(bf16[256,512]{0,1:T(8,128)(2,1)} %copy.143) | copy-start | bytes 786436
  58.1 1.3 %copy-start.5 = (bf16[256,512]{0,1:T(8,128)(2,1)S(1)}, bf16[256,512]{0,1:T(8,128)(2,1)}, u32[]{:S(2)}) copy-start(bf16[256,512]{0,1:T(8,128)(2,1)} %copy.147) | copy-start | bytes 786436
  62.1 1.0 %copy-start.10 = (bf16[256,512]{0,1:T(8,128)(2,1)S(1)}, bf16[256,512]{0,1:T(8,128)(2,1)}, u32[]{:S(2)}) copy-start(bf16[256,512]{0,1:T(8,128)(2,1)} %copy.144) | copy-start | bytes 786436
  65.1 2.2 %copy-start.9 = (bf16[256,512]{0,1:T(8,128)(2,1)S(1)}, bf16[256,512]{0,1:T(8,128)(2,1)}, u32[]{:S(2)}) copy-start(bf16[256,512]{0,1:T(8,128)(2,1)} %copy.145) | copy-start | bytes 786436
  74.3 4.3 %copy-start.3 = (f32[2048,1,128]{0,2,1:T(8,128)}, f32[2048,1,128]{0,2,1:T(8,128)S(1)}, u32[]{:S(2)}) copy-start(f32[2048,1,128]{0,2,1:T(8,128)S(1)} %fusion.51) | copy-start | bytes 3145732
  75.3 18.6 %collective-permute-start.1 = (bf16[1024,256]{0,1:T(8,128)(2,1)}, bf16[1024,256]{0,1:T(8,128)(2,1)}, u32[]{:S(2)}, u32[]{:S(2)}) collective-permute-start(bf16[1024,256]{0,1:T(8,128)(2,1)} %pad_maximum_fusion.3), channel_id=1, source_target_pairs={{8,0},{16,8},{24,16},{32,24},{40,32},{48,40},{56,48},{64,56},{72,6... | collective-permute-start | bytes 1572872 | tf_op jit(solution)/shard_map/ppermute | solution.py:14
  78.6 16.5 %copy-start.8 = (bf16[256,512]{0,1:T(8,128)(2,1)S(1)}, bf16[256,512]{0,1:T(8,128)(2,1)}, u32[]{:S(2)}) copy-start(bf16[256,512]{0,1:T(8,128)(2,1)} %copy.146) | copy-start | bytes 786436
  82.6 16.1 %copy-start.2 = (bf16[1,4,256,1024]{2,3,1,0:T(8,128)(2,1)S(1)}, bf16[1,4,256,1024]{2,3,1,0:T(8,128)(2,1)}, u32[]{:S(2)}) copy-start(bf16[1,4,256,1024]{2,3,1,0:T(8,128)(2,1)} %fusion.1) | copy-start | bytes 6291460
where the time goes:
time: 102 us; the launch traced here: 101 us
  matrix products  32 us (31%)
  local copies, waits for them, and re-layouts  21.8 us (21%)
  waiting for transfers between devices  19.1 us (19%)
  other arithmetic  15.4 us (15%)
  starting transfers between devices  11.8 us (12%)
  between operations  1.19 us (1%)
    ppermute x2, waiting for transfers between devices, from_behind(): return lax.ppermute(block, axis, route)  11.4 us
    unnamed x40, local copies, waits for them, and re-layouts  9.71 us
    all_to_all x1, waiting for transfers between devices, local(): lax.all_to_all(packed, 'head', split_axis=1, concat_axis=0, tiled=True)  7.72 us
    dot_general x4, matrix products, tile_grads(): jnp.einsum('grtn,ngd->tgrd', weights_low, value_rows, preferred_element_t...  7.66 us
    dot_general x4, matrix products, tile_grads(): jnp.einsum('grtn,tgrd->ngd', weights_low, grad_tile, preferred_element_ty...  7.63 us
    ppermute x2, starting transfers between devices, from_behind(): return lax.ppermute(block, axis, route)  7.29 us
    dot_general x4, matrix products, tile_grads(): jnp.einsum('tgrd,ngd->grtn', grad_tile, value_rows, preferred_element_typ...  6.65 us
    gather x1, other arithmetic, local(): prior_doc = jnp.repeat(prior_units, unit_rows, total_repeat_length=ctx_rows)  5.04 us
  transfers between devices with their start and end apart: 3, of which 2 were waited for; matrix products, arithmetic and copies ran while one was open for 32% of the time, Pallas kernels for 0%

commit v1 on v0

--- a/solution.py
+++ b/solution.py
@@ -62,7 +62,10 @@
         ],
         axis=2,
     )
-    packed = lax.all_to_all(packed, "head", split_axis=1, concat_axis=0, tiled=True)
+    packed = jnp.concatenate(
+        lax.all_to_all(jnp.stack(jnp.split(packed, lax.axis_size("head"), axis=1)), "head", 0, 0),
+        axis=0,
+    )
     ctx_rows = packed.shape[0]
     packed = packed.reshape(ctx_rows, q_cols + 2 * k_cols)
     kv_local = k_cols // HEAD_SIZE

time: 102 us -> 102 us (level)
  other arithmetic: 15.4 us -> 14.1 us
  waiting for transfers between devices: 19.1 us -> 20.2 us
    unnamed x40 -> x48, local copies, waits for them, and re-layouts: 9.71 us -> 12.8 us
    reshape x2 -> x0, local copies, waits for them, and re-layouts: 2.52 us -> none  [the longest x1 1.36 us: local(): query_matrix.reshape(token_per_shard, head_groups, q_cols)]
    concatenate x1, other arithmetic: 1.29 us -> 0.11 us  [local(): jnp.concatenate([query_matrix.reshape(token_per_shard, head_groups, q_col...]
    all_to_all x1, waiting for transfers between devices: 7.72 us -> 8.85 us  [local(): lax.all_to_all(jnp.stack(jnp.split(packed, lax.axis_size('head'), axis=1)...]
    another operation x4 -> x6, local copies, waits for them, and re-layouts: 3.12 us -> 4.04 us
  transfers between devices with their start and end apart: 3 -> 3, of which waited for: 2 -> 2; matrix products, arithmetic and copies ran while one was open for 32% -> 29% of each run, Pallas kernels for 0% -> 0%
where the time goes in v1:
time: 102 us
  matrix products  32 us (31%)
  local copies, waits for them, and re-layouts  22.2 us (22%)
  waiting for transfers between devices  20.2 us (20%)
  other arithmetic  14.1 us (14%)
  starting transfers between devices  11.8 us (12%)
  between operations  1.25 us (1%)
    unnamed x48, local copies, waits for them, and re-layouts  12.8 us
    ppermute x2, waiting for transfers between devices, from_behind(): return lax.ppermute(block, axis, route)  11.4 us
    all_to_all x1, waiting for transfers between devices, local(): lax.all_to_all(jnp.stack(jnp.split(packed, lax.axis_size('head'), axis=1)...  8.85 us
    dot_general x4, matrix products, tile_grads(): jnp.einsum('grtn,ngd->tgrd', weights_low, value_rows, preferred_element_t...  7.66 us
    dot_general x4, matrix products, tile_grads(): jnp.einsum('grtn,tgrd->ngd', weights_low, grad_tile, preferred_element_ty...  7.63 us
    ppermute x2, starting transfers between devices, from_behind(): return lax.ppermute(block, axis, route)  7.29 us
    dot_general x4, matrix products, tile_grads(): jnp.einsum('tgrd,ngd->grtn', grad_tile, value_rows, preferred_element_typ...  6.66 us
    gather x1, other arithmetic, local(): prior_doc = jnp.repeat(prior_units, unit_rows, total_repeat_length=ctx_rows)  4.99 us
  transfers between devices with their start and end apart: 3, of which 2 were waited for; matrix products, arithmetic and copies ran while one was open for 29% of the time, Pallas kernels for 0%

profile of v1, /device:TPU:102, one launch (start us, length us, event | category | flops | bytes accessed | tf_op | source)
XLA Modules:
  0.0 101.5 jit_solution(8498487329621340668)
XLA Ops:
  0.6 1.6 %copy.164 = bf16[128,4096]{0,1:T(8,128)(2,1)S(1)} copy(bf16[128,4096]{1,0:T(8,128)(2,1)} %param.27) | data formatting | bytes 2097152 | tf_op args[0]
  2.3 1.1 %copy.165 = bf16[128,1024]{0,1:T(8,128)(2,1)S(1)} copy(bf16[128,1024]{1,0:T(8,128)(2,1)} %param.28) | data formatting | bytes 524288 | tf_op args[1]
  3.4 1.1 %copy.166 = bf16[128,1024]{0,1:T(8,128)(2,1)S(1)} copy(bf16[128,1024]{1,0:T(8,128)(2,1)} %param.29) | data formatting | bytes 524288 | tf_op args[2]
  5.0 1.6 %copy.167 = bf16[8,128,1,768]{3,1,2,0:T(8,128)(2,1)} copy(bf16[8,128,1,768]{1,3,2,0:T(8,128)(2,1)S(1)} %fusion.166) | data formatting | bytes 3145728 | tf_op jit(solution)/shard_map/stack | solution.py:66
  6.6 4.5 %all-to-all-start = ((bf16[8,128,1,768]{3,1,2,0:T(8,128)(2,1)}), bf16[8,128,1,768]{3,1,2,0:T(8,128)(2,1)S(1)}, u32[]{:S(2)}, u32[]{:S(2)}) async-start(bf16[8,128,1,768]{3,1,2,0:T(8,128)(2,1)} %copy.167), calls=%async_computation | async-start | bytes 3145728 | tf_op jit(solution)/shard_map/all_to_all | solution.py:66
  11.2 0.2 reduce-window.9
  11.4 0.8 fusion.204
  12.1 0.1 select_reduce_fusion
  12.3 0.7 fusion.207
  13.0 5.0 %select_select_fusion.1 = (s32[1024]{0:T(1024)S(1)}, s32[1024]{0:T(1024)S(1)}) fusion(pred[1024]{0:T(1024)(128)(4,1)S(1)} %copy-done.11, pred[1024]{0:T(1024)(128)(4,1)S(1)} %copy-done.12, pred[1024]{0:T(1024)(128)(4,1)S(1)} %copy-done.13, s32[]{:T(128)} %bitcast.20, s32[]{:T(128)} %bitcast.19, s32[]{:T(128)} %bitcast.18, s32[]{:T(128)} %bitcast.17, ...), kind=kLoop, calls=%fused_computation.184 | loop fusion | flops 6144 | bytes 11296 | tf_op jit(solution)/shard_map/jit(_take)/gather | solution.py:91
  18.0 1.8 %copy.253 = bf16[256,512]{0,1:T(8,128)(2,1)} copy(bf16[256,512]{1,0:T(8,128)(2,1)} %get-tuple-element.145) | data formatting | bytes 524288
  19.8 0.9 copy.254
  20.6 0.9 copy.255
  21.5 0.8 copy.256
  22.4 0.3 fusion.136
  22.7 0.3 compare_and_fusion
  23.0 0.3 compare_and_fusion.2
  23.4 0.3 compare_and_fusion.1
  23.7 8.8 %all-to-all-done = bf16[8,128,1,768]{3,1,2,0:T(8,128)(2,1)S(1)} async-done(((bf16[8,128,1,768]{3,1,2,0:T(8,128)(2,1)}), bf16[8,128,1,768]{3,1,2,0:T(8,128)(2,1)S(1)}, u32[]{:S(2)}, u32[]{:S(2)}) %all-to-all-start) | async-done | bytes 1572896 | tf_op jit(solution)/shard_map/all_to_all | solution.py:66
  32.6 0.8 slice.388
  33.4 0.9 fusion.203
  34.3 5.1 %collective-permute-start = (bf16[1024,256]{1,0:T(8,128)(2,1)}, bf16[1024,256]{1,0:T(8,128)(2,1)}, u32[]{:S(2)}, u32[]{:S(2)}) collective-permute-start(bf16[1024,256]{1,0:T(8,128)(2,1)} %slice.388), channel_id=1, source_target_pairs={{0,8},{8,16},{16,24},{24,32},{32,40},{40,48},{48,56},{56,64},{64,7... | collective-permute-start | bytes 1572872 | tf_op jit(solution)/shard_map/ppermute | solution.py:14
  39.4 1.1 %copy.259 = bf16[256,512]{0,1:T(8,128)(2,1)S(1)} copy(bf16[256,512]{1,0:T(8,128)(2,1)} %get-tuple-element.140) | data formatting | bytes 524288 | tf_op jit(solution)/shard_map/reshape.304
  40.5 0.8 fusion.15
  41.3 0.9 exponential_reduce_fusion
  42.2 1.9 %fusion.141 = (f32[256,4]{0,1:T(4,128)S(1)}, bf16[256,1,4,128]{0,3,2,1:T(8,128)(2,1)}) fusion(bf16[256,1,4,128]{0,3,2,1:T(8,128)(2,1)S(1)} %bitcast.565, f32[1024,256,4]{1,0,2:T(8,128)S(1)} %get-tuple-element.173, f32[4,256]{1,0:T(4,128)S(1)} %log_add_fusion, pred[256,1024]{0,1:T(8,128)(4,1)S(1)} %compare_and_fusion, bf16[1024,768]{1,0:T(8,128)(2,1)S(1)} %bitcast.548), kind=kOutput, calls=%fused_computation.124 | convolution fusion | flops 273284096 | bytes 5251072 | tf_op jit(solution)/shard_map/grtn,ngd->tgrd/dot_general | solution.py:29
  44.2 2.7 %fusion.1 = bf16[1,4,256,1024]{2,3,1,0:T(8,128)(2,1)} fusion(f32[1024,256,4]{1,0,2:T(8,128)S(1)} %get-tuple-element.173, bf16[256,4,128]{0,2,1:T(8,128)(2,1)S(1)} %bitcast.566, f32[4,256]{1,0:T(4,128)S(1)} %bitcast.580, f32[4,256]{1,0:T(4,128)S(1)} %log_add_fusion, pred[256,1024]{0,1:T(8,128)(4,1)S(1)} %compare_and_fusion, bf16[1024,768]{1,0:T(8,128)(2,1)S(1)} %bitcast.549), kind=kOutput, calls=%fused_computation.2 | convolution fusion | flops 274726912 | bytes 7086080 | tf_op jit(solution)/shard_map/tgrd,ngd->grtn/dot_general | solution.py:34
  46.8 0.8 copy.169
  47.7 0.1 copy.257
  47.8 1.1 %copy.258 = bf16[256,512]{0,1:T(8,128)(2,1)S(1)} copy(bf16[256,512]{1,0:T(8,128)(2,1)} %get-tuple-element.141) | data formatting | bytes 524288 | tf_op jit(solution)/shard_map/reshape.295
  48.9 2.1 %fusion.129 = bf16[256,1,4,128]{0,3,2,1:T(8,128)(2,1)S(1)} fusion(bf16[1,4,256,1024]{2,3,1,0:T(8,128)(2,1)} %fusion.1, bf16[1024,768]{1,0:T(8,128)(2,1)S(1)} %bitcast.550), kind=kOutput, calls=%fused_computation.96 | convolution fusion | flops 268697600 | bytes 2621440 | tf_op jit(solution)/shard_map/grtn,ngd->tgrd/dot_general | solution.py:39
  51.1 1.1 %slice_bitcast_fusion = (bf16[1024,1,128]{2,0,1:T(8,128)(2,1)S(1)}, bf16[1024,1,128]{2,0,1:T(8,128)(2,1)S(1)}) fusion(bf16[1024,256]{1,0:T(8,128)(2,1)} %collective-permute-done), kind=kLoop, calls=%fused_computation.145 | loop fusion | bytes 1048576 | tf_op jit(solution)/shard_map/reshape | solution.py:79
  52.2 0.8 fusion.12
  52.9 0.9 exponential_reduce_fusion.3
  53.9 1.3 %convolution_bitcast_fusion.3 = f32[1024,1,128]{0,2,1:T(8,128)S(1)} fusion(bf16[256,4,128]{0,2,1:T(8,128)(2,1)S(1)} %bitcast.574, f32[1024,256,4]{1,0,2:T(8,128)S(1)} %get-tuple-element.179, f32[4,256]{1,0:T(4,128)S(1)} %log_add_fusion.3, pred[256,1024]{0,1:T(8,128)(4,1)S(1)} %fusion.136), kind=kOutput, calls=%fused_computation.60 | convolution fusion | flops 272629760 | bytes 5246976 | tf_op jit(solution)/shard_map/grtn,tgrd->ngd/dot_general | solution.py:46
  55.2 1.9 %fusion.144 = (f32[256,4]{0,1:T(4,128)S(1)}, bf16[256,1,4,128]{0,3,2,1:T(8,128)(2,1)}) fusion(bf16[256,1,4,128]{0,3,2,1:T(8,128)(2,1)S(1)} %bitcast.575, f32[1024,256,4]{1,0,2:T(8,128)S(1)} %get-tuple-element.179, f32[4,256]{1,0:T(4,128)S(1)} %log_add_fusion.3, pred[256,1024]{0,1:T(8,128)(4,1)S(1)} %fusion.136, ...), kind=kOutput, calls=%fused_computation.130 | convolution fusion | flops 273808384 | bytes 5513216 | tf_op jit(solution)/shard_map/grtn,ngd->tgrd/dot_general | solution.py:29
  57.1 1.3 %fusion.7 = bf16[1,4,256,1024]{2,3,1,0:T(8,128)(2,1)S(1)} fusion(f32[1024,256,4]{1,0,2:T(8,128)S(1)} %get-tuple-element.179, bf16[256,4,128]{0,2,1:T(8,128)(2,1)S(1)} %bitcast.576, f32[4,256]{1,0:T(4,128)S(1)} %bitcast.578, f32[4,256]{1,0:T(4,128)S(1)} %log_add_fusion.3, pred[256,1024]{0,1:T(8,128)(4,1)S(1)} %fusion.136, ...), kind=kOutput, calls=%fused_computation.11 | convolution fusion | flops 275251200 | bytes 7348224 | tf_op jit(solution)/shard_map/tgrd,ngd->grtn/dot_general | solution.py:34
  58.4 0.8 fusion.87
  59.2 0.5 fusion.120
  59.7 0.8 fusion.13
  60.5 1.1 %exponential_reduce_fusion.2 = f32[4,256]{1,0:T(4,128)S(1)} fusion(f32[1024,256,4]{1,0,2:T(8,128)S(1)} %get-tuple-element.177, f32[4,256]{1,0:T(4,128)S(1)} %get-tuple-element.176, pred[256,1024]{0,1:T(8,128)(4,1)S(1)} %compare_and_fusion.2), kind=kLoop, calls=%fused_computation.21 | loop fusion | flops 4193280 | bytes 4464640 | tf_op jit(solution)/shard_map/reduce_sum | solution.py:26
  61.7 0.8 fusion.14
  62.5 0.9 exponential_reduce_fusion.1
  63.5 1.9 %fusion.143 = (f32[256,4]{0,1:T(4,128)S(1)}, bf16[256,1,4,128]{0,3,2,1:T(8,128)(2,1)}) fusion(bf16[256,1,4,128]{0,3,2,1:T(8,128)(2,1)S(1)} %bitcast.571, f32[1024,256,4]{1,0,2:T(8,128)S(1)} %get-tuple-element.177, f32[4,256]{1,0:T(4,128)S(1)} %log_add_fusion.2, pred[256,1024]{0,1:T(8,128)(4,1)S(1)} %compare_and_fusion.2, ...), kind=kOutput, calls=%fused_computation.128 | convolution fusion | flops 273808384 | bytes 5513216 | tf_op jit(solution)/shard_map/grtn,ngd->tgrd/dot_general | solution.py:29
  65.4 1.3 %fusion.5 = bf16[1,4,256,1024]{2,3,1,0:T(8,128)(2,1)S(1)} fusion(f32[1024,256,4]{1,0,2:T(8,128)S(1)} %get-tuple-element.177, bf16[256,4,128]{0,2,1:T(8,128)(2,1)S(1)} %bitcast.572, f32[4,256]{1,0:T(4,128)S(1)} %bitcast.581, f32[4,256]{1,0:T(4,128)S(1)} %log_add_fusion.2, pred[256,1024]{0,1:T(8,128)(4,1)S(1)} %compare_and_fusion.2, ...), kind=kOutput, calls=%fused_computation.8 | convolution fusion | flops 275251200 | bytes 7348224 | tf_op jit(solution)/shard_map/tgrd,ngd->grtn/dot_general | solution.py:34
  66.7 0.9 fusion.93
  67.6 1.9 %fusion.142 = (f32[256,4]{0,1:T(4,128)S(1)}, bf16[256,1,4,128]{0,3,2,1:T(8,128)(2,1)}) fusion(bf16[256,1,4,128]{0,3,2,1:T(8,128)(2,1)S(1)} %bitcast.568, f32[1024,256,4]{1,0,2:T(8,128)S(1)} %get-tuple-element.175, f32[4,256]{1,0:T(4,128)S(1)} %log_add_fusion.1, pred[256,1024]{0,1:T(8,128)(4,1)S(1)} %compare_and_fusion.1, ...), kind=kOutput, calls=%fused_computation.126 | convolution fusion | flops 273808384 | bytes 5513216 | tf_op jit(solution)/shard_map/grtn,ngd->tgrd/dot_general | solution.py:29
  69.5 1.3 %fusion.3 = bf16[1,4,256,1024]{2,3,1,0:T(8,128)(2,1)S(1)} fusion(f32[1024,256,4]{1,0,2:T(8,128)S(1)} %get-tuple-element.175, bf16[256,4,128]{0,2,1:T(8,128)(2,1)S(1)} %bitcast.569, f32[4,256]{1,0:T(4,128)S(1)} %bitcast.579, f32[4,256]{1,0:T(4,128)S(1)} %log_add_fusion.1, pred[256,1024]{0,1:T(8,128)(4,1)S(1)} %compare_and_fusion.1, ...), kind=kOutput, calls=%fused_computation.5 | convolution fusion | flops 275251200 | bytes 7348224 | tf_op jit(solution)/shard_map/tgrd,ngd->grtn/dot_general | solution.py:34
  70.9 0.9 fusion.99
  71.9 1.4 %fusion.49 = f32[2048,1,128]{0,2,1:T(8,128)S(1)} fusion(f32[2048,1,128]{0,2,1:T(8,128)S(1)} %scatter-add.25, bf16[256,4,128]{0,2,1:T(8,128)(2,1)S(1)} %bitcast.573, f32[1024,256,4]{1,0,2:T(8,128)S(1)} %get-tuple-element.177, f32[4,256]{1,0:T(4,128)S(1)} %log_add_fusion.2, pred[256,1024]{0,1:T(8,128)(4,1)S(1)} %compare_and_fusion.2), kind=kOutput, calls=%fused_computation.62 | convolution fusion | flops 272760832 | bytes 5771264 | tf_op jit(solution)/shard_map/grtn,tgrd->ngd/dot_general | solution.py:46
  73.3 1.4 %fusion.51 = f32[2048,1,128]{0,2,1:T(8,128)S(1)} fusion(f32[2048,1,128]{0,2,1:T(8,128)S(1)} %fusion.49, bf16[256,4,128]{0,2,1:T(8,128)(2,1)S(1)} %bitcast.570, f32[1024,256,4]{1,0,2:T(8,128)S(1)} %get-tuple-element.175, f32[4,256]{1,0:T(4,128)S(1)} %log_add_fusion.1, pred[256,1024]{0,1:T(8,128)(4,1)S(1)} %compare_and_fusion.1), kind=kOutput, calls=%fused_computation.64 | convolution fusion | flops 272760832 | bytes 5771264 | tf_op jit(solution)/shard_map/grtn,tgrd->ngd/dot_general | solution.py:46
  74.7 0.9 pad_maximum_fusion.3
  75.6 2.2 %collective-permute-start.1 = (bf16[1024,256]{0,1:T(8,128)(2,1)}, bf16[1024,256]{0,1:T(8,128)(2,1)}, u32[]{:S(2)}, u32[]{:S(2)}) collective-permute-start(bf16[1024,256]{0,1:T(8,128)(2,1)} %pad_maximum_fusion.3), channel_id=1, source_target_pairs={{8,0},{16,8},{24,16},{32,24},{40,32},{48,40},{56,48},{64,56},{72,6... | collective-permute-start | bytes 1572872 | tf_op jit(solution)/shard_map/ppermute | solution.py:14
  77.8 0.5 fusion.126
  78.3 0.5 fusion.123
  78.9 1.3 %copy.211 = bf16[1024,512]{1,0:T(8,128)(2,1)} copy(bf16[1024,512]{0,1:T(8,128)(2,1)S(1)} %bitcast.553) | data formatting | bytes 2097152
  80.3 1.2 %pad_maximum_fusion.1 = bf16[1024,1,4,128]{0,3,2,1:T(8,128)(2,1)S(1)} fusion(bf16[256,1,4,128]{0,3,2,1:T(8,128)(2,1)S(1)} %copy-done.10, bf16[256,1,4,128]{0,3,2,1:T(8,128)(2,1)} %get-tuple-element.183, bf16[256,1,4,128]{0,3,2,1:T(8,128)(2,1)} %get-tuple-element.185, bf16[256,1,4,128]{0,3,2,1:T(8,128)(2,1)} %get-tuple-element.187), kind=kLoop, calls=%fused_computation.101 | loop fusion | flops 4194304 | bytes 2097152 | tf_op jit(solution)/shard_map/concatenate | solution.py:137
  81.5 1.3 %copy.210 = bf16[1024,512]{1,0:T(8,128)(2,1)} copy(bf16[1024,512]{0,1:T(8,128)(2,1)S(1)} %bitcast.554) | data formatting | bytes 2097152
  82.8 11.4 %collective-permute-done.1 = bf16[1024,256]{0,1:T(8,128)(2,1)} collective-permute-done((bf16[1024,256]{0,1:T(8,128)(2,1)}, bf16[1024,256]{0,1:T(8,128)(2,1)}, u32[]{:S(2)}, u32[]{:S(2)}) %collective-permute-start.1) | collective-permute-done | bytes 524320 | tf_op jit(solution)/shard_map/ppermute | solution.py:14
  94.2 1.1 %convert_element_type.219 = f32[1024,256]{0,1:T(8,128)S(1)} convert(bf16[1024,256]{0,1:T(8,128)(2,1)} %collective-permute-done.1) | non-fusion elementwise | flops 262144 | bytes 1572864 | tf_op jit(solution)/shard_map/convert_element_type | solution.py:132
  95.4 3.6 %fusion.137 = bf16[1024,128]{0,1:T(8,128)(2,1)S(1)} fusion(f32[1024,256]{0,1:T(8,128)S(1)} %convert_element_type.219, bf16[256,4,128]{0,2,1:T(8,128)(2,1)S(1)} %bitcast.567, f32[2048,1,128]{0,2,1:T(8,128)} %copy-done.2, f32[1024,256,4]{1,0,2:T(8,128)} %copy-done, f32[4,256]{1,0:T(4,128)S(1)} %log_add_fusion, pred[256,1024]{0,1:T(8,128)(4,1)S(1)} %compare_and_fusion), kind=kOutput, calls=%fused_computation.117 | convolution fusion | flops 273022976 | bytes 6033408 | tf_op jit(solution)/shard_map/grtn,tgrd->ngd/dot_general | solution.py:46
  99.0 0.8 fusion.138
  99.8 0.8 copy.213
  100.7 0.8 copy.212
  (58 shorter events, 1.0 us)
Async XLA Ops:
  4.7 6.3 %copy-start.14 = (s32[128]{0:T(128)S(1)}, s32[128]{0:T(128)}, u32[]{:S(2)}) copy-start(s32[128]{0:T(128)} %param.31) | copy-start | bytes 1540
  4.7 6.6 %copy-start.3 = (bf16[1024,512]{1,0:T(8,128)(2,1)S(1)}, bf16[1024,512]{1,0:T(8,128)(2,1)}, u32[]{:S(2)}) copy-start(bf16[1024,512]{1,0:T(8,128)(2,1)} %param.30) | copy-start | bytes 3145732
  4.9 8.0 %copy-start.11 = (pred[1024]{0:T(1024)(128)(4,1)S(1)}, pred[1024]{0:T(1024)(128)(4,1)}, u32[]{:S(2)}) copy-start(pred[1024]{0:T(1024)(128)(4,1)} %constant.343) | copy-start | bytes 3076
  4.9 8.0 %copy-start.12 = (pred[1024]{0:T(1024)(128)(4,1)S(1)}, pred[1024]{0:T(1024)(128)(4,1)}, u32[]{:S(2)}) copy-start(pred[1024]{0:T(1024)(128)(4,1)} %constant.344) | copy-start | bytes 3076
  5.0 8.0 %copy-start.13 = (pred[1024]{0:T(1024)(128)(4,1)S(1)}, pred[1024]{0:T(1024)(128)(4,1)}, u32[]{:S(2)}) copy-start(pred[1024]{0:T(1024)(128)(4,1)} %constant.345) | copy-start | bytes 3076
  6.6 26.0 %all-to-all-start = ((bf16[8,128,1,768]{3,1,2,0:T(8,128)(2,1)}), bf16[8,128,1,768]{3,1,2,0:T(8,128)(2,1)S(1)}, u32[]{:S(2)}, u32[]{:S(2)}) async-start(bf16[8,128,1,768]{3,1,2,0:T(8,128)(2,1)} %copy.167), calls=%async_computation | async-start | bytes 3145728 | tf_op jit(solution)/shard_map/all_to_all | solution.py:66
  34.3 16.8 %collective-permute-start = (bf16[1024,256]{1,0:T(8,128)(2,1)}, bf16[1024,256]{1,0:T(8,128)(2,1)}, u32[]{:S(2)}, u32[]{:S(2)}) collective-permute-start(bf16[1024,256]{1,0:T(8,128)(2,1)} %slice.388), channel_id=1, source_target_pairs={{0,8},{8,16},{16,24},{24,32},{32,40},{40,48},{48,56},{56,64},{64,7... | collective-permute-start | bytes 1572872 | tf_op jit(solution)/shard_map/ppermute | solution.py:14
  40.5 1.7 %copy-start.5 = (bf16[256,512]{0,1:T(8,128)(2,1)S(1)}, bf16[256,512]{0,1:T(8,128)(2,1)}, u32[]{:S(2)}) copy-start(bf16[256,512]{0,1:T(8,128)(2,1)} %copy.256) | copy-start | bytes 786436
  41.3 2.9 %copy-start = (f32[1024,256,4]{1,0,2:T(8,128)}, f32[1024,256,4]{1,0,2:T(8,128)S(1)}, u32[]{:S(2)}) copy-start(f32[1024,256,4]{1,0,2:T(8,128)S(1)} %get-tuple-element.173) | copy-start | bytes 12582916
  48.9 3.2 %copy-start.4 = (bf16[256,512]{0,1:T(8,128)(2,1)S(1)}, bf16[256,512]{0,1:T(8,128)(2,1)}, u32[]{:S(2)}) copy-start(bf16[256,512]{0,1:T(8,128)(2,1)} %copy.169) | copy-start | bytes 786436
  52.1 1.7 %copy-start.9 = (bf16[256,512]{0,1:T(8,128)(2,1)S(1)}, bf16[256,512]{0,1:T(8,128)(2,1)}, u32[]{:S(2)}) copy-start(bf16[256,512]{0,1:T(8,128)(2,1)} %copy.253) | copy-start | bytes 786436
  62.5 1.0 %copy-start.8 = (bf16[256,512]{0,1:T(8,128)(2,1)S(1)}, bf16[256,512]{0,1:T(8,128)(2,1)}, u32[]{:S(2)}) copy-start(bf16[256,512]{0,1:T(8,128)(2,1)} %copy.254) | copy-start | bytes 786436
  65.4 2.2 %copy-start.7 = (bf16[256,512]{0,1:T(8,128)(2,1)S(1)}, bf16[256,512]{0,1:T(8,128)(2,1)}, u32[]{:S(2)}) copy-start(bf16[256,512]{0,1:T(8,128)(2,1)} %copy.255) | copy-start | bytes 786436
  74.6 4.3 %copy-start.2 = (f32[2048,1,128]{0,2,1:T(8,128)}, f32[2048,1,128]{0,2,1:T(8,128)S(1)}, u32[]{:S(2)}) copy-start(f32[2048,1,128]{0,2,1:T(8,128)S(1)} %fusion.51) | copy-start | bytes 3145732
  75.6 18.6 %collective-permute-start.1 = (bf16[1024,256]{0,1:T(8,128)(2,1)}, bf16[1024,256]{0,1:T(8,128)(2,1)}, u32[]{:S(2)}, u32[]{:S(2)}) collective-permute-start(bf16[1024,256]{0,1:T(8,128)(2,1)} %pad_maximum_fusion.3), channel_id=1, source_target_pairs={{8,0},{16,8},{24,16},{32,24},{40,32},{48,40},{56,48},{64,56},{72,6... | collective-permute-start | bytes 1572872 | tf_op jit(solution)/shard_map/ppermute | solution.py:14
  78.3 2.0 %copy-start.10 = (bf16[256,1,4,128]{0,3,2,1:T(8,128)(2,1)S(1)}, bf16[256,1,4,128]{0,3,2,1:T(8,128)(2,1)}, u32[]{:S(2)}) copy-start(bf16[256,1,4,128]{0,3,2,1:T(8,128)(2,1)} %get-tuple-element.181) | copy-start | bytes 786436
  78.9 16.5 %copy-start.6 = (bf16[256,512]{0,1:T(8,128)(2,1)S(1)}, bf16[256,512]{0,1:T(8,128)(2,1)}, u32[]{:S(2)}) copy-start(bf16[256,512]{0,1:T(8,128)(2,1)} %copy.256) | copy-start | bytes 786436
  82.8 16.2 %copy-start.1 = (bf16[1,4,256,1024]{2,3,1,0:T(8,128)(2,1)S(1)}, bf16[1,4,256,1024]{2,3,1,0:T(8,128)(2,1)}, u32[]{:S(2)}) copy-start(bf16[1,4,256,1024]{2,3,1,0:T(8,128)(2,1)} %fusion.1) | copy-start | bytes 6291460
